TPU v7x, 128 devices: a whole 4x4x4 slice. The times are simulated.
128 devices in a mesh: tile: 32 (over x_lo, y, z), src: 4 (over x_hi, core).
Axes of the slice: x: 4 (x_hi: 2, x_lo: 2; x = x_hi * 2 + x_lo), y: 4, z: 4, core: 2. Of those that a mesh axis runs over, the one named last changes fastest.
Arguments:
- tile_tokens: bfloat16 [32768, 2048], P(('tile', 'src')), may hold values from -6 to 6
- norm_gain: float32 [2048], replicated, may hold values from 0.25 to 2.5
- up_weight: bfloat16 [2048, 2816], P('tile'), may hold values from -0.125 to 0.125
- down_weight: bfloat16 [2816, 2048], P('tile'), may hold values from -0.109375 to 0.109375
- head_weight: bfloat16 [2048, 768], P(None, 'src'), may hold values from -0.125 to 0.125
- source_index: int32 [128, 2], replicated, may hold values from 0 to 96, as said below
- source_cutoff: int32 [128], replicated, may hold values from 8 to 16
- source_weight: float32 [128], replicated, may hold values from 0.3 to 3
Outputs:
- intensity: float32 [128, 4096], P(('tile', 'src'))
Inputs may be any that keep to these rules, and one draw needn't show every extreme that they name: `source_index`: in each aligned group of 4 source points the first has the least value of the group in both coordinates, the second lies exactly 32 beyond it in both, and every other lies within 32 of the first in both.
All inputs are finite; a program needn't handle non-finite values.
Results may differ from a plain program's by a relative error of at most 0.0007.
Values may be sent and summed in bfloat16 or wider, within the bound.
No kernel may reach another device: no remote copies, remote signals or barrier semaphores. Data moves between devices by JAX's collectives and lax.ppermute only.
A program may use at most 128 MiB of HBM per device.

v0:
```python
import math
import jax
import jax.numpy as jnp
from jax import lax
from jax.sharding import PartitionSpec as P

GRID = 16
SUB = 8
W = 32
REG = 64
PIX = 64
SRC_DEV = 4
PATCH = 256
ORD = 128
f32 = jnp.float32
bf16 = jnp.bfloat16


def split_bf16(x):
    hi = lax.reduce_precision(x, exponent_bits=8, mantissa_bits=7)
    lo = x - hi
    return (hi.astype(bf16), lo.astype(bf16))


def phase_tables():
    turn = 2.0 * math.pi / PIX
    v = jnp.arange(ORD, dtype=jnp.int32)
    y = jnp.arange(PIX, dtype=jnp.int32)
    ang = jnp.mod(v[:, None] * y[None, :], PIX).astype(f32) * turn
    cv, sv = (jnp.cos(ang), jnp.sin(ang))
    t1 = jnp.stack([jnp.concatenate([cv, sv], 1), jnp.concatenate([-sv, cv], 1)], 0)
    i = jnp.arange(W, dtype=jnp.int32)
    x = jnp.arange(PIX, dtype=jnp.int32)
    ang2 = jnp.mod(x[:, None] * i[None, :], PIX).astype(f32) * turn
    ca, sa = (jnp.cos(ang2), jnp.sin(ang2))
    t2 = jnp.stack([jnp.stack([ca, -sa], 1), jnp.stack([sa, ca], 1)], 0)
    return (t1, t2)


def imaging(spec, source_index, source_cutoff, source_weight):
    T = spec.shape[0]
    S = source_index.shape[0]
    x0 = jnp.clip(source_index[:, 0], 0, ORD - W)
    y0 = jnp.clip(source_index[:, 1], 0, ORD - W)
    rows = x0[:, None] + jnp.arange(W, dtype=jnp.int32)[None, :]
    pick = (rows[:, :, None] == jnp.arange(ORD, dtype=jnp.int32)[None, None, :]).astype(bf16)
    spec_rows = spec.reshape(T, 6, 2, ORD, ORD)
    strips = jnp.einsum("siu,tkpuv->sitkpv", pick, spec_rows, preferred_element_type=f32).astype(
        bf16
    )
    i = jnp.arange(W, dtype=jnp.int32)
    j = jnp.arange(ORD, dtype=jnp.int32)[None, :] - y0[:, None]
    dist = (i[None, :, None] - W // 2) ** 2 + (j[:, None, :] - W // 2) ** 2
    keep = (
        (dist <= (source_cutoff * source_cutoff)[:, None, None])
        & (j[:, None, :] >= 0)
        & (j[:, None, :] < W)
    )
    masked = jnp.where(keep[:, :, None, None, None, :], strips, jnp.zeros((), bf16))
    t1, t2 = phase_tables()
    half = jnp.einsum("sitkpv,pvn->sitkn", masked.astype(f32), t1, precision=lax.Precision.HIGH)
    half = half.reshape(S, W, T, 6, 2, PIX)
    field = jnp.einsum("cxqi,sitkqy->tskcxy", t2, half, precision=lax.Precision.HIGH)
    power = jnp.sum(field * field * source_weight[None, :, None, None, None, None], axis=(1, 2, 3))
    return power.reshape(T, PIX * PIX) * (1.0 / (6.0 * W * W * S))


def local(
    tile_tokens,
    norm_gain,
    up_weight,
    down_weight,
    head_weight,
    source_index,
    source_cutoff,
    source_weight,
):
    token_count, d_model = tile_tokens.shape
    n_tile = lax.axis_size("tile")
    n_src = lax.axis_size("src")
    me = lax.axis_index("src")
    half = me % 2
    up_rows, ff = up_weight.shape
    down_rows = down_weight.shape[0]
    up_half, down_half = (up_rows // 2, down_rows // 2)
    depth = -(-(up_half + down_half) // 16) * 16
    width = max(ff, d_model)
    up_part = lax.dynamic_slice_in_dim(up_weight, half * up_half, up_half, 0)
    down_part = lax.dynamic_slice_in_dim(down_weight, half * down_half, down_half, 0)
    packed = jnp.concatenate(
        [
            jnp.pad(up_part, ((0, 0), (0, width - ff))),
            jnp.pad(down_part, ((0, depth - up_half - down_half), (0, width - d_model))),
        ],
        0,
    )
    gathered = lax.all_gather(packed, "tile", axis=0, tiled=True)
    sibling = lax.ppermute(gathered, "src", [(s, s ^ 1) for s in range(n_src)])
    head_parts = [head_weight] + [
        lax.ppermute(head_weight, "src", [(s, s ^ k) for s in range(n_src)])
        for k in range(1, n_src)
    ]
    residual = tile_tokens.astype(jnp.float32)
    mean_square = jnp.mean(residual * residual, axis=1, keepdims=True)
    normed = (residual * lax.rsqrt(mean_square + 1e-05) * norm_gain).astype(jnp.bfloat16)

    def spread(x, rows, start):
        view = x.reshape(x.shape[0], n_tile, 2, rows // 2)
        pad = ((0, 0), (0, 0), (start, depth - start - rows // 2))
        mine = jnp.pad(lax.dynamic_index_in_dim(view, half, 2, keepdims=False), pad)
        other = jnp.pad(lax.dynamic_index_in_dim(view, 1 - half, 2, keepdims=False), pad)
        return (mine.reshape(x.shape[0], -1), other.reshape(x.shape[0], -1))

    normed_mine, normed_other = spread(normed, up_rows, 0)
    pre_act = jnp.dot(normed_mine, gathered, preferred_element_type=jnp.float32) + jnp.dot(
        normed_other, sibling, preferred_element_type=jnp.float32
    )
    hidden = jax.nn.gelu(pre_act[:, :ff]).astype(jnp.bfloat16)
    hidden_mine, hidden_other = spread(hidden, down_rows, up_half)
    branch_out = jnp.dot(hidden_mine, gathered, preferred_element_type=jnp.float32) + jnp.dot(
        hidden_other, sibling, preferred_element_type=jnp.float32
    )
    branch_out = branch_out[:, :d_model]
    mixed = (residual + branch_out).astype(jnp.bfloat16)
    parts = jnp.stack(head_parts, 0)
    coeff_parts = jnp.einsum(
        "tk,pkc->ptc", mixed, parts, preferred_element_type=jnp.float32
    ).astype(jnp.bfloat16)
    order = me ^ jnp.arange(n_src, dtype=jnp.int32)
    coeffs = jnp.take(coeff_parts, order, axis=0).transpose(1, 0, 2).reshape(token_count, -1)
    tile_count = token_count // PATCH
    spectra = (
        coeffs.reshape(tile_count, GRID, GRID, 12, SUB, SUB)
        .transpose(0, 3, 1, 4, 2, 5)
        .reshape(tile_count, 12, ORD, ORD)
    )
    return imaging(spectra, source_index, source_cutoff, source_weight)


def solution(mesh):
    return jax.shard_map(
        local,
        mesh=mesh,
        in_specs=(
            P(("tile", "src"), None),
            P(),
            P("tile", None),
            P("tile", None),
            P(None, "src"),
            P(),
            P(),
            P(),
        ),
        out_specs=P(("tile", "src"), None),
        check_vma=False,
    )
```

profile of v0, /device:TPU:1, one launch (start us, length us, event | category | flops | bytes accessed | tf_op | source)
XLA Modules:
  0.0 335.5 jit_solution(13254922369213393428)
XLA Ops:
  6.6 1.0 copy-done
  7.6 0.9 constant_dynamic-slice_fusion.1
  8.5 0.8 fusion.45
  9.3 170.6 %all-gather.2.cloned.1.call-done = bf16[2560,2816]{1,0:T(8,128)(2,1)} async-done(((bf16[80,2816]{1,0:T(8,128)(2,1)}), bf16[2560,2816]{1,0:T(8,128)(2,1)}) %all-gather.2.cloned.1.call-update) | async-done | bytes 14417936 | tf_op jit(solution)/shard_map/all_gather | solution.py:97
  179.9 15.1 %collective-permute-start.3 = (bf16[2560,2816]{1,0:T(8,128)(2,1)}, bf16[2560,2816]{1,0:T(8,128)(2,1)}, u32[]{:S(2)}, u32[]{:S(2)}) collective-permute-start(bf16[2560,2816]{1,0:T(8,128)(2,1)} %all-gather.2.cloned.1.call-done), channel_id=1, source_target_pairs={{0,1},{1,0},{2,3},{3,2},{4,5},{5,4},{6,7},{7,6},{8,9},{9,8},{10,11... | collective-permute-start | bytes 43253768 | tf_op jit(solution)/shard_map/ppermute | solution.py:98
  195.0 3.1 collective-permute-start.1
  198.6 1.5 fusion.26
  203.2 2.4 fusion.31
  205.6 7.6 %fusion.72 = f32[256,2816]{1,0:T(8,128)S(1)} fusion(bf16[256,2560]{0,1:T(8,128)(2,1)S(1)} %bitcast.100, bf16[2560,2816]{1,0:T(8,128)(2,1)} %all-gather.2.cloned.1.call-done), kind=kOutput, calls=%fused_computation.107 | convolution fusion | flops 3690987520 | bytes 18612224 | tf_op jit(solution)/shard_map/dot_general | solution.py:115
  213.2 3.5 %collective-permute-done.3 = bf16[2560,2816]{1,0:T(8,128)(2,1)} collective-permute-done((bf16[2560,2816]{1,0:T(8,128)(2,1)}, bf16[2560,2816]{1,0:T(8,128)(2,1)}, u32[]{:S(2)}, u32[]{:S(2)}) %collective-permute-start.3) | collective-permute-done | bytes 14417952 | tf_op jit(solution)/shard_map/ppermute | solution.py:98
  216.7 9.9 %fusion.25 = bf16[256,2816]{1,0:T(8,128)(2,1)S(1)} fusion(f32[256,2816]{1,0:T(8,128)S(1)} %fusion.72, bf16[256,2560]{0,1:T(8,128)(2,1)S(1)} %bitcast.104, bf16[2560,2816]{1,0:T(8,128)(2,1)} %collective-permute-done.3), kind=kOutput, calls=%fused_computation.31 | convolution fusion | flops 3698196480 | bytes 20054016 | tf_op jit(solution)/shard_map/dot_general | solution.py:115
  226.7 0.7 copy.28
  228.0 7.6 %fusion.73 = f32[256,2816]{1,0:T(8,128)S(1)} fusion(bf16[256,2560]{0,1:T(8,128)(2,1)S(1)} %bitcast.101, bf16[2560,2816]{1,0:T(8,128)(2,1)} %all-gather.2.cloned.1.call-done), kind=kOutput, calls=%fused_computation.108 | convolution fusion | flops 3690987520 | bytes 18612224 | tf_op jit(solution)/shard_map/dot_general | solution.py:120
  235.7 7.9 %fusion.74 = f32[256,2816]{1,0:T(8,128)S(1)} fusion(bf16[256,2560]{0,1:T(8,128)(2,1)S(1)} %bitcast.102, bf16[2560,2816]{1,0:T(8,128)(2,1)} %collective-permute-done.3), kind=kOutput, calls=%fused_computation.109 | convolution fusion | flops 3690987520 | bytes 18612224 | tf_op jit(solution)/shard_map/dot_general | solution.py:120
  243.7 2.7 fusion.38
  246.9 0.9 select_bitcast_fusion
  247.8 3.5 %reshape_reshape.4 = bf16[1,16,16,12,8,8]{2,1,5,4,3,0:T(8,128)(2,1)S(1)} reshape(bf16[256,4,192]{0,2,1:T(8,128)(2,1)} %select_bitcast_fusion) | data formatting | bytes 786432 | tf_op jit(solution)/shard_map/reshape;reshape | solution.py:133
  251.3 5.3 %copy.33 = bf16[1,16,16,12,8,8]{5,2,4,1,3,0:T(8,128)(2,1)} copy(bf16[1,16,16,12,8,8]{2,1,5,4,3,0:T(8,128)(2,1)S(1)} %reshape_reshape.4) | data formatting | bytes 786432 | tf_op jit(solution)/shard_map/reshape;reshape | solution.py:133
  256.6 8.2 %reshape.276 = bf16[6,2,128,128,1]{3,2,1,0,4:T(8,128)(2,1)S(1)} reshape(bf16[1,12,16,8,16,8]{5,4,3,2,1,0:T(8,128)(2,1)} %bitcast.99) | data formatting | bytes 786432 | tf_op jit(solution)/shard_map/reshape.2
  264.8 6.5 %fusion.33 = bf16[128,32,6,2,128]{4,1,3,2,0:T(8,128)(2,1)} fusion(bf16[6,2,128,128,1]{3,2,1,0,4:T(8,128)(2,1)S(1)} %reshape.276, s32[128,32]{1,0:T(8,128)S(1)} %iota_add_fusion), kind=kOutput, calls=%fused_computation.42 | convolution fusion | flops 1611137024 | bytes 12992512 | tf_op jit(solution)/shard_map/siu,tkpuv->sitkpv/dot_general | solution.py:48
  271.3 14.6 %fusion.6 = f32[128,32,6,2,64,1]{4,1,3,2,0,5:T(8,128)} fusion(f32[2,64,2,128,1,1]{3,1,0,2,5,4:T(8,128)S(1)} %bitcast.105, bf16[128,32,6,2,128]{4,1,3,2,0:T(8,128)(2,1)} %fusion.33, pred[128,32,128]{2,1,0:T(8,128)(4,1)S(1)} %copy-done.2), kind=kOutput, calls=%fused_computation.9 | convolution fusion | flops 4838129664 | bytes 25821184 | tf_op jit(solution)/shard_map/sitkpv,pvn->sitkn/dot_general | solution.py:61
  286.0 22.9 %copy.42 = f32[128,32,6,2,64,1]{0,1,3,5,4,2:T(8,128)} copy(f32[128,32,6,2,64,1]{4,1,3,2,0,5:T(8,128)} %fusion.6) | data formatting | bytes 25165824 | tf_op jit(solution)/shard_map/sitkpv,pvn->sitkn/dot_general | solution.py:61
  308.8 19.0 %fusion = f32[64,64]{1,0:T(8,128)S(1)} fusion(f32[128]{0:T(128)S(1)} %copy-done.10, f32[128,32,6,2,64,1]{0,1,3,5,4,2:T(8,128)} %copy.42, f32[1,64,2,32]{1,3,2,0:T(8,128)S(1)} %copy-done.5, f32[1,64,2,32]{1,3,2,0:T(8,128)S(1)} %get-tuple-element.11), kind=kOutput, calls=%fused_computation.2 | convolution fusion | flops 2434797568 | bytes 12632576 | tf_op jit(solution)/shard_map/cxqi,sitkqy->tskcxy/dot_general | solution.py:63
  328.0 0.7 mul.233
  (58 shorter events, 4.8 us)
Async XLA Ops:
  6.5 1.0 copy-start
  6.5 193.6 %copy-start.3 = (bf16[256,2048]{1,0:T(8,128)(2,1)S(1)}, bf16[256,2048]{1,0:T(8,128)(2,1)}, u32[]{:S(2)}) copy-start(bf16[256,2048]{1,0:T(8,128)(2,1)} %param.8) | copy-start | bytes 3145732
  6.5 193.6 %copy-start.6 = (f32[2048]{0:T(1024)S(1)}, f32[2048]{0:T(1024)}, u32[]{:S(2)}) copy-start(f32[2048]{0:T(1024)} %param.9) | copy-start | bytes 24580
  6.5 173.4 %all-gather.2.cloned.1.call-start = ((), (), s32[]{:S(2)}) async-start(), calls=%async_computation | async-start | bytes 14868480 | tf_op jit(solution)/shard_map/all_gather | solution.py:97
  179.9 36.8 %collective-permute-start.3 = (bf16[2560,2816]{1,0:T(8,128)(2,1)}, bf16[2560,2816]{1,0:T(8,128)(2,1)}, u32[]{:S(2)}, u32[]{:S(2)}) collective-permute-start(bf16[2560,2816]{1,0:T(8,128)(2,1)} %all-gather.2.cloned.1.call-done), channel_id=1, source_target_pairs={{0,1},{1,0},{2,3},{3,2},{4,5},{5,4},{6,7},{7,6},{8,9},{9,8},{10,11... | collective-permute-start | bytes 43253768 | tf_op jit(solution)/shard_map/ppermute | solution.py:98
  195.0 48.6 %collective-permute-start = (bf16[2048,192]{0,1:T(8,128)(2,1)}, bf16[2048,192]{0,1:T(8,128)(2,1)}, u32[]{:S(2)}, u32[]{:S(2)}) collective-permute-start(bf16[2048,192]{0,1:T(8,128)(2,1)} %param.12), channel_id=1, source_target_pairs={{0,1},{1,0},{2,3},{3,2},{4,5},{5,4},{6,7},{7,6},{8,9},{9,8},{10,11... | collective-permute-start | bytes 2359304 | tf_op jit(solution)/shard_map/ppermute | solution.py:100
  195.0 48.6 %collective-permute-start.1 = (bf16[2048,192]{0,1:T(8,128)(2,1)}, bf16[2048,192]{0,1:T(8,128)(2,1)}, u32[]{:S(2)}, u32[]{:S(2)}) collective-permute-start(bf16[2048,192]{0,1:T(8,128)(2,1)} %param.12), channel_id=1, source_target_pairs={{0,2},{1,3},{2,0},{3,1},{4,6},{5,7},{6,4},{7,5},{8,10},{9,11},{10,... | collective-permute-start | bytes 2359304 | tf_op jit(solution)/shard_map/ppermute | solution.py:100
  198.1 45.5 %collective-permute-start.2 = (bf16[2048,192]{0,1:T(8,128)(2,1)}, bf16[2048,192]{0,1:T(8,128)(2,1)}, u32[]{:S(2)}, u32[]{:S(2)}) collective-permute-start(bf16[2048,192]{0,1:T(8,128)(2,1)} %param.12), channel_id=1, source_target_pairs={{0,3},{1,2},{2,1},{3,0},{4,7},{5,6},{6,5},{7,4},{8,11},{9,10},{10,... | collective-permute-start | bytes 2359304 | tf_op jit(solution)/shard_map/ppermute | solution.py:100
  201.0 0.7 copy-start.9
  201.0 1.8 copy-start.7
  235.6 8.0 %copy-start.4 = (bf16[256,2048]{1,0:T(8,128)(2,1)S(1)}, bf16[256,2048]{1,0:T(8,128)(2,1)}, u32[]{:S(2)}) copy-start(bf16[256,2048]{1,0:T(8,128)(2,1)} %param.8) | copy-start | bytes 3145732
  235.7 8.0 %copy-start.8 = (bf16[2048,192]{0,1:T(8,128)(2,1)S(1)}, bf16[2048,192]{0,1:T(8,128)(2,1)}, u32[]{:S(2)}) copy-start(bf16[2048,192]{0,1:T(8,128)(2,1)} %param.12) | copy-start | bytes 2359300
  264.8 6.5 %copy-start.2 = (pred[128,32,128]{2,1,0:T(8,128)(4,1)S(1)}, pred[128,32,128]{2,1,0:T(8,128)(4,1)}, u32[]{:S(2)}) copy-start(pred[128,32,128]{2,1,0:T(8,128)(4,1)} %fusion.31) | copy-start | bytes 1572868
  285.9 22.9 %copy-start.5 = (f32[1,64,2,32]{1,3,2,0:T(8,128)S(1)}, f32[1,64,2,32]{1,3,2,0:T(8,128)}, u32[]{:S(2)}) copy-start(f32[1,64,2,32]{1,3,2,0:T(8,128)} %get-tuple-element.12) | copy-start | bytes 49156
  285.9 22.9 %copy-start.10 = (f32[128]{0:T(128)S(1)}, f32[128]{0:T(128)}, u32[]{:S(2)}) copy-start(f32[128]{0:T(128)} %param.15) | copy-start | bytes 1540
  308.8 19.8 %copy-start.1 = (bf16[88,2048]{1,0:T(8,128)(2,1)S(1)}, bf16[88,2048]{1,0:T(8,128)(2,1)}, u32[]{:S(2)}) copy-start(bf16[88,2048]{1,0:T(8,128)(2,1)} %param.11) | copy-start | bytes 1081348
Sparse Core Ops, SparseCore 0:
  9.5 170.4 all-gather.1
where the time goes:
time: 336 us
  waiting for transfers between devices  174 us (52%)
  matrix products  75.9 us (23%)
  local copies, waits for them, and re-layouts  45.7 us (14%)
  starting transfers between devices  18.7 us (6%)
  between operations  13.8 us (4%)
  other arithmetic  7.29 us (2%)
    all_gather x1, waiting for transfers between devices, local(): gathered = lax.all_gather(packed, 'tile', axis=0, tiled=True)  171 us
    dot_general x1, local copies, waits for them, and re-layouts, imaging(): jnp.einsum('sitkpv,pvn->sitkn', masked.astype(f32), t1, precision=lax.Pre...  22.9 us
    dot_general x1, matrix products, imaging(): jnp.einsum('cxqi,sitkqy->tskcxy', t2, half, precision=lax.Precision.HIGH)  19 us
    ppermute x1, starting transfers between devices, local(): sibling = lax.ppermute(gathered, 'src', [(s, s ^ 1) for s in range(n_src)])  15.1 us
    dot_general x1, matrix products, imaging(): jnp.einsum('sitkpv,pvn->sitkn', masked.astype(f32), t1, precision=lax.Pre...  14.6 us
    dot_general x1, matrix products, local(): jnp.dot(normed_other, sibling, preferred_element_type=jnp.float32)  9.91 us
    another operation x2, local copies, waits for them, and re-layouts, local(): coeffs.reshape(tile_count, GRID, GRID, 12, SUB, SUB)  8.8 us
    another operation x1, local copies, waits for them, and re-layouts  8.2 us
  transfers between devices with their start and end apart: 5, of which 2 were waited for; matrix products, arithmetic and copies ran while one was open for 12% of the time, Pallas kernels for 0%

commit v1 on v0

--- a/solution.py
+++ b/solution.py
@@ -94,7 +94,9 @@
         ],
         0,
     )
-    gathered = lax.all_gather(packed, "tile", axis=0, tiled=True)
+    gathered = jnp.concatenate(
+        lax.all_to_all(jnp.stack([packed] * lax.axis_size("tile")), "tile", 0, 0), axis=0
+    )
     sibling = lax.ppermute(gathered, "src", [(s, s ^ 1) for s in range(n_src)])
     head_parts = [head_weight] + [
         lax.ppermute(head_weight, "src", [(s, s ^ k) for s in range(n_src)])

time: 336 us -> 320 us (0.952)
  blocking collectives: 0 us -> 173 us
  waiting for transfers between devices: 174 us -> 5.23 us
  between operations: 13.8 us -> 0.36 us
  starting transfers between devices: 18.7 us -> 5.38 us
  local copies, waits for them, and re-layouts: 45.7 us -> 51 us
    all_to_all x0 -> x1, blocking collectives: none -> 173 us  [local(): lax.all_to_all(jnp.stack([packed] * lax.axis_size('tile')), 'tile', 0, 0)]
    all_gather x1 -> x0, waiting for transfers between devices: 171 us -> none  [local(): gathered = lax.all_gather(packed, 'tile', axis=0, tiled=True)]
    ppermute x1, starting transfers between devices: 15.1 us -> 1.74 us  [local(): sibling = lax.ppermute(gathered, 'src', [(s, s ^ 1) for s in range(n_src)])]
    another operation x1 -> x2, local copies, waits for them, and re-layouts: 8.2 us -> 14.2 us
  transfers between devices with their start and end apart: 5 -> 4, of which waited for: 2 -> 1; matrix products, arithmetic and copies ran while one was open for 12% -> 13% of each run, Pallas kernels for 0% -> 0%
where the time goes in v1:
time: 320 us; the launch traced here: 319 us
  blocking collectives  173 us (54%)
  matrix products  78.7 us (25%)
  local copies, waits for them, and re-layouts  51 us (16%)
  starting transfers between devices  5.38 us (2%)
  other arithmetic  5.28 us (2%)
  waiting for transfers between devices  5.23 us (2%)
    all_to_all x1, blocking collectives, local(): lax.all_to_all(jnp.stack([packed] * lax.axis_size('tile')), 'tile', 0, 0)  173 us
    dot_general x1, local copies, waits for them, and re-layouts, imaging(): jnp.einsum('sitkpv,pvn->sitkn', masked.astype(f32), t1, precision=lax.Pre...  22.7 us
    dot_general x1, matrix products, imaging(): jnp.einsum('cxqi,sitkqy->tskcxy', t2, half, precision=lax.Precision.HIGH)  19 us
    dot_general x1, matrix products, imaging(): jnp.einsum('sitkpv,pvn->sitkn', masked.astype(f32), t1, precision=lax.Pre...  14.6 us
    dot_general x1, matrix products, local(): jnp.dot(hidden_mine, gathered, preferred_element_type=jnp.float32)  10.5 us
    dot_general x1, matrix products, local(): jnp.dot(normed_other, sibling, preferred_element_type=jnp.float32)  9.91 us
    another operation x2, local copies, waits for them, and re-layouts, local(): coeffs.reshape(tile_count, GRID, GRID, 12, SUB, SUB)  8.8 us
    another operation x1, local copies, waits for them, and re-layouts  8.2 us
  transfers between devices with their start and end apart: 4, of which 1 were waited for; matrix products, arithmetic and copies ran while one was open for 13% of the time, Pallas kernels for 0%

profile of v1, /device:TPU:1, one launch (start us, length us, event | category | flops | bytes accessed | tf_op | source)
XLA Modules:
  0.0 319.2 jit_solution(6835644848222443638)
XLA Ops:
  0.0 1.0 copy-done
  1.0 0.9 constant_dynamic-slice_fusion.2
  2.0 6.0 %stack.33 = bf16[32,80,2816]{2,1,0:T(8,128)(2,1)} broadcast(bf16[80,2816]{1,0:T(8,128)(2,1)S(1)} %fusion.53), dimensions={1,2} | broadcast | bytes 14868480 | tf_op jit(solution)/shard_map/stack | solution.py:98
  8.0 173.2 %all_to_all.5 = bf16[32,80,2816]{2,1,0:T(8,128)(2,1)} all-to-all(bf16[32,80,2816]{2,1,0:T(8,128)(2,1)} %stack.33), channel_id=1, replica_groups=mesh['tile'=32,'src'=4] {'tile'}, dimensions={0} | all-to-all | bytes 28835840 | tf_op jit(solution)/shard_map/all_to_all | solution.py:98
  181.3 1.7 collective-permute-start.3
  183.0 2.5 collective-permute-start.1
  185.5 1.2 collective-permute-start.2
  189.5 2.4 fusion.36
  191.9 7.6 %convolution_bitcast_fusion = f32[256,2816]{1,0:T(8,128)S(1)} fusion(bf16[32,80,2816]{2,1,0:T(8,128)(2,1)} %all_to_all.5, bf16[256,32,32]{0,2,1:T(8,128)(2,1)S(1)} %get-tuple-element.8), kind=kOutput, calls=%fused_computation.14 | convolution fusion | flops 3690987520 | bytes 17825792 | tf_op jit(solution)/shard_map/dot_general | solution.py:117
  199.5 5.2 %collective-permute-done.3 = bf16[2560,2816]{1,0:T(8,128)(2,1)} collective-permute-done((bf16[2560,2816]{1,0:T(8,128)(2,1)}, bf16[2560,2816]{1,0:T(8,128)(2,1)}, u32[]{:S(2)}, u32[]{:S(2)}) %collective-permute-start.3) | collective-permute-done | bytes 14417952 | tf_op jit(solution)/shard_map/ppermute | solution.py:100
  204.8 9.9 %fusion.30 = bf16[256,2816]{1,0:T(8,128)(2,1)S(1)} fusion(f32[256,2816]{1,0:T(8,128)S(1)} %convolution_bitcast_fusion, bf16[256,2560]{0,1:T(8,128)(2,1)S(1)} %bitcast.102, bf16[2560,2816]{1,0:T(8,128)(2,1)} %collective-permute-done.3), kind=kOutput, calls=%fused_computation.35 | convolution fusion | flops 3698196480 | bytes 20054016 | tf_op jit(solution)/shard_map/dot_general | solution.py:117
  214.7 0.7 copy.28
  215.9 7.6 %fusion.81 = f32[256,2816]{1,0:T(8,128)S(1)} fusion(bf16[256,2560]{0,1:T(8,128)(2,1)S(1)} %bitcast.100, bf16[2560,2816]{1,0:T(8,128)(2,1)} %collective-permute-done.3), kind=kOutput, calls=%fused_computation.115 | convolution fusion | flops 3690987520 | bytes 18612224 | tf_op jit(solution)/shard_map/dot_general | solution.py:122
  223.6 10.5 %fusion.12 = f32[256,2816]{1,0:T(8,128)S(1)} fusion(bf16[32,80,2816]{2,1,0:T(8,128)(2,1)} %all_to_all.5, bf16[256,32,1,44]{0,3,2,1:T(8,128)(2,1)S(1)} %get-tuple-element.5), kind=kOutput, calls=%fused_computation.15 | convolution fusion | flops 2030043136 | bytes 18022400 | tf_op jit(solution)/shard_map/dot_general | solution.py:122
  234.1 3.0 fusion.44
  237.6 0.8 select_bitcast_fusion
  238.5 3.5 %reshape_reshape.4 = bf16[1,16,16,12,8,8]{2,1,5,4,3,0:T(8,128)(2,1)S(1)} reshape(bf16[256,4,192]{0,2,1:T(8,128)(2,1)} %select_bitcast_fusion) | data formatting | bytes 786432 | tf_op jit(solution)/shard_map/reshape;reshape | solution.py:135
  242.0 5.3 %copy.33 = bf16[1,16,16,12,8,8]{5,2,4,1,3,0:T(8,128)(2,1)} copy(bf16[1,16,16,12,8,8]{2,1,5,4,3,0:T(8,128)(2,1)S(1)} %reshape_reshape.4) | data formatting | bytes 786432 | tf_op jit(solution)/shard_map/reshape;reshape | solution.py:135
  247.3 8.2 %reshape.278 = bf16[6,2,128,128,1]{3,2,1,0,4:T(8,128)(2,1)S(1)} reshape(bf16[1,12,16,8,16,8]{5,4,3,2,1,0:T(8,128)(2,1)} %bitcast.99) | data formatting | bytes 786432 | tf_op jit(solution)/shard_map/reshape.3
  255.5 6.5 %fusion.38 = bf16[128,32,6,2,128]{4,1,3,2,0:T(8,128)(2,1)} fusion(bf16[6,2,128,128,1]{3,2,1,0,4:T(8,128)(2,1)S(1)} %reshape.278, s32[128,32]{1,0:T(8,128)S(1)} %iota_add_fusion), kind=kOutput, calls=%fused_computation.46 | convolution fusion | flops 1611137024 | bytes 12992512 | tf_op jit(solution)/shard_map/siu,tkpuv->sitkpv/dot_general | solution.py:48
  262.0 14.6 %fusion.8 = f32[128,32,6,2,64,1]{4,1,3,2,0,5:T(8,128)} fusion(f32[2,64,2,128,1,1]{3,1,0,2,5,4:T(8,128)S(1)} %bitcast.103, bf16[128,32,6,2,128]{4,1,3,2,0:T(8,128)(2,1)} %fusion.38, pred[128,32,128]{2,1,0:T(8,128)(4,1)S(1)} %copy-done.2), kind=kOutput, calls=%fused_computation.11 | convolution fusion | flops 4838129664 | bytes 25821184 | tf_op jit(solution)/shard_map/sitkpv,pvn->sitkn/dot_general | solution.py:61
  276.6 22.7 %copy.42 = f32[128,32,6,2,64,1]{0,1,3,5,4,2:T(8,128)} copy(f32[128,32,6,2,64,1]{4,1,3,2,0,5:T(8,128)} %fusion.8) | data formatting | bytes 25165824 | tf_op jit(solution)/shard_map/sitkpv,pvn->sitkn/dot_general | solution.py:61
  299.3 19.0 %fusion = f32[64,64]{1,0:T(8,128)S(1)} fusion(f32[128]{0:T(128)S(1)} %copy-done.9, f32[128,32,6,2,64,1]{0,1,3,5,4,2:T(8,128)} %copy.42, f32[1,64,2,32]{1,3,2,0:T(8,128)S(1)} %copy-done.5, f32[1,64,2,32]{1,3,2,0:T(8,128)S(1)} %get-tuple-element.11), kind=kOutput, calls=%fused_computation.2 | convolution fusion | flops 2434797568 | bytes 12632576 | tf_op jit(solution)/shard_map/cxqi,sitkqy->tskcxy/dot_general | solution.py:63
  318.4 0.7 mul.233
  (53 shorter events, 4.0 us)
Async XLA Ops:
  0.0 1.0 copy-start
  8.0 178.6 %copy-start.3 = (bf16[256,2048]{1,0:T(8,128)(2,1)S(1)}, bf16[256,2048]{1,0:T(8,128)(2,1)}, u32[]{:S(2)}) copy-start(bf16[256,2048]{1,0:T(8,128)(2,1)} %param.8) | copy-start | bytes 3145732
  8.0 178.9 %copy-start.6 = (f32[2048]{0:T(1024)S(1)}, f32[2048]{0:T(1024)}, u32[]{:S(2)}) copy-start(f32[2048]{0:T(1024)} %param.9) | copy-start | bytes 24580
  181.3 6.5 %copy-start.8 = (s32[128]{0:T(128)S(1)}, s32[128]{0:T(128)}, u32[]{:S(2)}) copy-start(s32[128]{0:T(128)} %param.14) | copy-start | bytes 1540
  181.3 23.5 %collective-permute-start.3 = (bf16[2560,2816]{1,0:T(8,128)(2,1)}, bf16[2560,2816]{1,0:T(8,128)(2,1)}, u32[]{:S(2)}, u32[]{:S(2)}) collective-permute-start(bf16[2560,2816]{1,0:T(8,128)(2,1)} %bitcast.13), channel_id=1, source_target_pairs={{0,1},{1,0},{2,3},{3,2},{4,5},{5,4},{6,7},{7,6},{8,9},{9,8},{10,11... | collective-permute-start | bytes 43253768 | tf_op jit(solution)/shard_map/ppermute | solution.py:100
  183.0 51.0 %collective-permute-start = (bf16[2048,192]{0,1:T(8,128)(2,1)}, bf16[2048,192]{0,1:T(8,128)(2,1)}, u32[]{:S(2)}, u32[]{:S(2)}) collective-permute-start(bf16[2048,192]{0,1:T(8,128)(2,1)} %param.12), channel_id=1, source_target_pairs={{0,1},{1,0},{2,3},{3,2},{4,5},{5,4},{6,7},{7,6},{8,9},{9,8},{10,11... | collective-permute-start | bytes 2359304 | tf_op jit(solution)/shard_map/ppermute | solution.py:102
  183.0 51.0 %collective-permute-start.1 = (bf16[2048,192]{0,1:T(8,128)(2,1)}, bf16[2048,192]{0,1:T(8,128)(2,1)}, u32[]{:S(2)}, u32[]{:S(2)}) collective-permute-start(bf16[2048,192]{0,1:T(8,128)(2,1)} %param.12), channel_id=1, source_target_pairs={{0,2},{1,3},{2,0},{3,1},{4,6},{5,7},{6,4},{7,5},{8,10},{9,11},{10,... | collective-permute-start | bytes 2359304 | tf_op jit(solution)/shard_map/ppermute | solution.py:102
  185.5 48.6 %collective-permute-start.2 = (bf16[2048,192]{0,1:T(8,128)(2,1)}, bf16[2048,192]{0,1:T(8,128)(2,1)}, u32[]{:S(2)}, u32[]{:S(2)}) collective-permute-start(bf16[2048,192]{0,1:T(8,128)(2,1)} %param.12), channel_id=1, source_target_pairs={{0,3},{1,2},{2,1},{3,0},{4,7},{5,6},{6,5},{7,4},{8,11},{9,10},{10,... | collective-permute-start | bytes 2359304 | tf_op jit(solution)/shard_map/ppermute | solution.py:102
  187.8 1.4 copy-start.7
  223.6 10.5 %copy-start.4 = (bf16[256,2048]{1,0:T(8,128)(2,1)S(1)}, bf16[256,2048]{1,0:T(8,128)(2,1)}, u32[]{:S(2)}) copy-start(bf16[256,2048]{1,0:T(8,128)(2,1)} %param.8) | copy-start | bytes 3145732
  255.5 6.5 %copy-start.2 = (pred[128,32,128]{2,1,0:T(8,128)(4,1)S(1)}, pred[128,32,128]{2,1,0:T(8,128)(4,1)}, u32[]{:S(2)}) copy-start(pred[128,32,128]{2,1,0:T(8,128)(4,1)} %fusion.36) | copy-start | bytes 1572868
  276.6 22.7 %copy-start.5 = (f32[1,64,2,32]{1,3,2,0:T(8,128)S(1)}, f32[1,64,2,32]{1,3,2,0:T(8,128)}, u32[]{:S(2)}) copy-start(f32[1,64,2,32]{1,3,2,0:T(8,128)} %get-tuple-element.12) | copy-start | bytes 49156
  276.6 22.7 %copy-start.9 = (f32[128]{0:T(128)S(1)}, f32[128]{0:T(128)}, u32[]{:S(2)}) copy-start(f32[128]{0:T(128)} %param.15) | copy-start | bytes 1540
  299.3 19.8 %copy-start.1 = (bf16[88,2048]{1,0:T(8,128)(2,1)S(1)}, bf16[88,2048]{1,0:T(8,128)(2,1)}, u32[]{:S(2)}) copy-start(bf16[88,2048]{1,0:T(8,128)(2,1)} %param.11) | copy-start | bytes 1081348
